TPU v7x, 32 devices: a whole 2x2x4 slice. The times are simulated.
32 devices in a mesh: lat: 8 (over y, x, core), lon: 4 (over z).
Axes of the slice: x: 2, y: 2, z: 4, core: 2. Of those that a mesh axis runs over, the one named last changes fastest.
Arguments:
- spec_coef: bfloat16 [1280, 2, 64, 1280], P(('lat', 'lon')), may hold values from -0.119628906 to 0.119628906
- legendre: bfloat16 [1280, 128, 1280], P(('lat', 'lon')), may hold values from -0.15625 to 0.15625
- wave_ids: int32 [1280], replicated, may hold values from 0 to 1279, each once
- dep_drow: int32 [128, 5120], P('lat', 'lon'), may hold values from -1 to 1
- dep_dlon: int32 [128, 5120], P('lat', 'lon'), may hold values from -1 to 1
- dep_frac: float32 [2, 128, 5120], P(None, 'lat', 'lon'), may hold values from 0 to 1
Outputs:
- grid: bfloat16 [64, 128, 5120], P(None, 'lat', 'lon')
- departed: bfloat16 [64, 128, 5120], P(None, 'lat', 'lon')
Inputs may be any that keep to these rules, and one draw needn't show every extreme that they name: `wave_ids`: each zonal wavenumber 0 to 1279 stands in exactly one storage row.
All inputs are finite; a program needn't handle non-finite values.
Results may differ from a plain program's by a relative error of at most 0.0059.
Values may be sent and summed in bfloat16 or wider, within the bound.
No kernel may reach another device: no remote copies, remote signals or barrier semaphores. Data moves between devices by JAX's collectives and lax.ppermute only.
A program may use at most 128 MiB of HBM per device.

v0:
```python
import math
import jax
import jax.numpy as jnp
from jax import lax
from jax.sharding import PartitionSpec as P

REACH = 1


def padded_2(cells, sides, width, closed):
    for axis, dim in sides:
        count = lax.axis_size(axis)
        ends = count if closed else count - 1
        head = lax.slice_in_dim(cells, 0, width, axis=dim)
        tail = lax.slice_in_dim(cells, cells.shape[dim] - width, cells.shape[dim], axis=dim)
        cells = jnp.concatenate(
            [
                lax.ppermute(tail, axis, [(i, (i + 1) % count) for i in range(ends)]),
                cells,
                lax.ppermute(head, axis, [((i + 1) % count, i) for i in range(ends)]),
            ],
            axis=dim,
        )
    return cells


def wave_table(wave_order, lon_start, lon_count, cycle_size):
    longitude = lon_start + jnp.arange(lon_count, dtype=jnp.int32)
    phase_index = wave_order[:, None] * longitude[None, :] % cycle_size
    theta = phase_index.astype(jnp.float32) * (2.0 * math.pi / cycle_size)
    factor = jnp.where(wave_order == 0, 1.0, 2.0).astype(jnp.float32)[:, None]
    return jnp.stack([factor * jnp.cos(theta), -factor * jnp.sin(theta)]).astype(jnp.bfloat16)


def shift_weight(offsets, frac, shift):
    zeros = jnp.zeros_like(frac)
    lower = jnp.where(offsets == shift, 1.0 - frac, zeros)
    higher = jnp.where(offsets == shift - 1, frac, zeros)
    return lower + higher


def per_device(spec_coef, legendre, wave_ids, dep_drow, dep_dlon, dep_frac):
    lat_count = lax.axis_size("lat")
    lon_parts = lax.axis_size("lon")
    local_waves = spec_coef.shape[0]
    level_fields = spec_coef.shape[2]
    degree_count = spec_coef.shape[3]
    all_waves = wave_ids.shape[0]
    row_count = dep_drow.shape[0]
    sector_width = dep_drow.shape[1]
    cycle_size = sector_width * lon_parts
    quarter = level_fields // lon_parts
    device = lax.axis_index("lat") * lon_parts + lax.axis_index("lon")
    local_ids = lax.dynamic_slice_in_dim(wave_ids, device * local_waves, local_waves)
    keep = jnp.arange(degree_count, dtype=jnp.int32)[None, :] >= local_ids[:, None]
    kept = jnp.where(keep[:, None, None, :], spec_coef, jnp.zeros((), spec_coef.dtype))
    kept = kept.reshape(local_waves, 2, lon_parts, quarter, degree_count)
    matrices = legendre.reshape(local_waves, lat_count, row_count, degree_count)
    fourier = jnp.einsum(
        "mrbqn,mapn->mabprq", kept, matrices, preferred_element_type=jnp.float32
    ).astype(jnp.bfloat16)
    moved = lax.all_to_all(
        lax.all_to_all(fourier, "lat", split_axis=1, concat_axis=0, tiled=True),
        "lon",
        split_axis=2,
        concat_axis=0,
        tiled=True,
    )
    wave_order = (
        wave_ids.reshape(lat_count, lon_parts, local_waves).transpose(1, 0, 2).reshape(all_waves)
    )
    moved = moved.reshape(all_waves, row_count, 2, quarter)
    table = wave_table(wave_order, lax.axis_index("lon") * sector_width, sector_width, cycle_size)
    grid = jnp.einsum(
        "mprq,rmx->qpx",
        lax.all_gather(moved, "lon", axis=3, tiled=True),
        table,
        preferred_element_type=jnp.float32,
    ).astype(jnp.bfloat16)
    margin = REACH + 1
    tall = padded_2(grid, (("lat", 1),), margin, False)
    padded = padded_2(tall, (("lon", 2),), margin, True)
    frac_row = dep_frac[0]
    frac_col = dep_frac[1]
    col_weights = [shift_weight(dep_dlon, frac_col, shift) for shift in range(-REACH, REACH + 2)]
    total = jnp.zeros((level_fields, row_count, sector_width), jnp.float32)
    for row_shift in range(-REACH, REACH + 2):
        band = padded[:, margin + row_shift : margin + row_shift + row_count, :]
        along = jnp.zeros((level_fields, row_count, sector_width), jnp.float32)
        for place, col_shift in enumerate(range(-REACH, REACH + 2)):
            window = band[:, :, margin + col_shift : margin + col_shift + sector_width].astype(
                jnp.float32
            )
            along = along + col_weights[place][None] * window
        total = total + shift_weight(dep_drow, frac_row, row_shift)[None] * along
    return (grid, total.astype(jnp.bfloat16))


def solution(mesh):
    in_specs = (
        P(("lat", "lon"), None, None, None),
        P(("lat", "lon"), None, None),
        P(),
        P("lat", "lon"),
        P("lat", "lon"),
        P(None, "lat", "lon"),
    )
    out_specs = (P(None, "lat", "lon"), P(None, "lat", "lon"))
    return jax.shard_map(
        per_device, mesh=mesh, in_specs=in_specs, out_specs=out_specs, check_vma=False
    )
```

profile of v0, /device:TPU:5, one launch (start us, length us, event | category | flops | bytes accessed | tf_op | source)
XLA Modules:
  0.0 315.4 jit_solution(18104308854111554694)
XLA Ops:
  7.2 0.8 dynamic_slice.3
  8.0 0.1 iota_compare_fusion
  8.1 7.0 %broadcast_select_fusion = bf16[40,2,64,1280]{3,2,1,0:T(8,128)(2,1)S(1)} fusion(bf16[40,2,64,1280]{3,2,1,0:T(8,128)(2,1)} %param.6, pred[40,1280]{1,0:T(8,128)(4,1)S(1)} %iota_compare_fusion), kind=kLoop, calls=%fused_computation | loop fusion | flops 6553600 | bytes 26265600 | tf_op jit(solution)/shard_map/jit(_where)/select_n | solution.py:56
  15.1 19.7 %convert_bitcast_fusion = bf16[40,8,4,16,2,16]{3,5,1,2,4,0:T(8,128)(2,1)} fusion(bf16[40,2,4,16,1280,1]{4,3,5,2,1,0:T(8,128)(2,1)S(1)} %bitcast.93, bf16[40,8,16,1280,1,1]{3,2,1,5,4,0:T(8,128)(2,1)} %bitcast.97), kind=kOutput, calls=%fused_computation.1 | convolution fusion | flops 1678376960 | bytes 27525120 | tf_op jit(solution)/shard_map/mrbqn,mapn->mabprq/dot_general | solution.py:59
  34.9 17.7 %copy.20 = bf16[40,8,4,16,2,16]{0,5,4,3,2,1:T(8,128)(2,1)} copy(bf16[40,8,4,16,2,16]{3,5,1,2,4,0:T(8,128)(2,1)} %convert_bitcast_fusion) | data formatting | bytes 2621440 | tf_op jit(solution)/shard_map/convert_element_type | solution.py:61
  52.6 8.1 %reshape.245 = bf16[8,2,40960]{2,1,0:T(2,128)(2,1)S(1)} reshape(bf16[8,4,16,2,16,40]{5,4,3,2,1,0:T(8,128)(2,1)} %bitcast.92) | data formatting | bytes 2621440
  60.7 20.0 %all_to_all.33 = bf16[8,2,40960]{2,1,0:T(2,128)(2,1)S(1)} all-to-all(bf16[8,2,40960]{2,1,0:T(2,128)(2,1)S(1)} %reshape.245), channel_id=1, replica_groups=mesh['lat'=8,'lon'=4] {'lat'}, dimensions={0} | all-to-all | bytes 2621440 | tf_op jit(solution)/shard_map/all_to_all | solution.py:63
  80.7 7.2 %reshape.246 = bf16[8,4,16,2,16,40]{5,4,3,2,1,0:T(8,128)(2,1)} reshape(bf16[8,2,40960]{2,1,0:T(2,128)(2,1)S(1)} %all_to_all.33) | data formatting | bytes 2621440
  87.9 3.0 bitcast_bitcast_fusion
  90.9 6.8 %copy.21 = bf16[8,40,1,4,16,2,16]{1,0,6,5,4,3,2:T(8,128)(2,1)} copy(bf16[8,40,1,4,16,2,16]{1,6,5,4,3,0,2:T(8,128)(2,1)S(1)} %bitcast_bitcast_fusion) | data formatting | bytes 2621440 | tf_op jit(solution)/shard_map/all_to_all | solution.py:63
  97.7 5.5 %all_to_all.27 = bf16[320,1,4,16,2,16]{0,5,4,3,2,1:T(8,128)(2,1)S(1)} reshape(bf16[8,40,1,4,16,2,16]{1,0,6,5,4,3,2:T(8,128)(2,1)} %copy.21) | data formatting | bytes 2621440 | tf_op jit(solution)/shard_map/all_to_all | solution.py:63
  103.2 40.5 %all_to_all.34 = bf16[320,1,4,16,2,16]{0,5,4,3,1,2:T(8,128)(2,1)S(1)} all-to-all(bf16[320,1,4,16,2,16]{0,5,4,3,1,2:T(8,128)(2,1)S(1)} %bitcast.95), channel_id=1, replica_groups=mesh['lat'=8,'lon'=4] {'lon'}, dimensions={2} | all-to-all | bytes 2621440 | tf_op jit(solution)/shard_map/all_to_all | solution.py:62
  143.8 1.2 copy.23
  145.0 2.1 reshape.240
  147.1 0.1 reshape.236
  147.2 0.1 reshape.237
  147.3 29.5 %multiply_convert_fusion.1 = (bf16[1,1280,1280]{2,1,0:T(8,128)(2,1)S(1)}, bf16[1,1280,1280]{2,1,0:T(8,128)(2,1)}) fusion(s32[1280]{0:T(1024)S(1)} %iota_add_fusion, s32[1280]{0:T(1024)S(1)} %reshape.237, f32[1280]{0:T(1024)S(1)} %get-tuple-element.30, f32[1280]{0:T(1024)S(1)} %get-tuple-element.31), kind=kLoop, calls=%fused_computation.10 | loop fusion | flops 21299200 | bytes 6574080 | tf_op jit(solution)/shard_map/convert
  176.8 68.7 %all-gather.2.cloned.1.call-done = bf16[1280,16,2,64]{0,3,2,1:T(8,128)(2,1)} async-done(((bf16[1280,16,2,16]{0,3,2,1:T(8,128)(2,1)}), bf16[1280,16,2,64]{0,3,2,1:T(8,128)(2,1)}) %all-gather.2.cloned.1.call-update) | async-done | bytes 5242896 | tf_op jit(solution)/shard_map/all_gather | solution.py:76
  245.6 9.9 %fusion.8 = bf16[64,16,1280]{2,0,1:T(8,128)(2,1)S(1)} fusion(bf16[1280,16,2,64]{0,3,2,1:T(8,128)(2,1)} %all-gather.2.cloned.1.call-done, bf16[1,1280,1280]{2,1,0:T(8,128)(2,1)} %get-tuple-element.29, bf16[1,1280,1280]{2,1,0:T(8,128)(2,1)S(1)} %get-tuple-element.28), kind=kOutput, calls=%fused_computation.19 | convolution fusion | flops 6725304320 | bytes 14417920 | tf_op jit(solution)/shard_map/mprq,rmx->qpx/dot_general | solution.py:74
  255.6 3.6 %collective-permute-start = (bf16[64,2,1280]{2,0,1:T(8,128)(2,1)S(1)}, bf16[64,2,1280]{2,0,1:T(8,128)(2,1)S(1)}, u32[]{:S(2)}, u32[]{:S(2)}) collective-permute-start(bf16[64,2,1280]{2,0,1:T(8,128)(2,1)S(1)} %get-tuple-element.14), channel_id=1, source_target_pairs={{0,4},{4,8},{8,12},{12,16},{16,20},{20,24},{24,28},{1,5},{5,9},{9,... | collective-permute-start | bytes 983048 | tf_op jit(solution)/shard_map/ppermute | solution.py:18
  259.2 1.9 collective-permute-start.1
  261.1 2.1 collective-permute-done
  263.2 4.4 %collective-permute-done.1 = bf16[64,2,1280]{2,0,1:T(8,128)(2,1)S(1)} collective-permute-done((bf16[64,2,1280]{2,0,1:T(8,128)(2,1)S(1)}, bf16[64,2,1280]{2,0,1:T(8,128)(2,1)S(1)}, u32[]{:S(2)}, u32[]{:S(2)}) %collective-permute-start.1) | collective-permute-done | bytes 327712 | tf_op jit(solution)/shard_map/ppermute | solution.py:20
  267.6 0.2 pad_maximum_fusion.5
  267.8 3.3 %collective-permute-start.3 = (bf16[64,20,2]{2,0,1:T(8,128)(2,1)S(1)}, bf16[64,20,2]{2,0,1:T(8,128)(2,1)S(1)}, u32[]{:S(2)}, u32[]{:S(2)}) collective-permute-start(bf16[64,20,2]{2,0,1:T(8,128)(2,1)S(1)} %get-tuple-element.13), channel_id=1, source_target_pairs={{1,0},{2,1},{3,2},{0,3},{5,4},{6,5},{7,6},{4,7},{9,8},{10,9},{11,1... | collective-permute-start | bytes 15368 | tf_op jit(solution)/shard_map/ppermute | solution.py:20
  271.1 0.1 fusion.14
  271.2 2.9 copy.24
  274.1 5.1 %collective-permute-done.2 = bf16[64,20,2]{2,0,1:T(8,128)(2,1)S(1)} collective-permute-done((bf16[64,20,2]{2,0,1:T(8,128)(2,1)S(1)}, bf16[64,20,2]{2,0,1:T(8,128)(2,1)S(1)}, u32[]{:S(2)}, u32[]{:S(2)}) %collective-permute-start.2) | collective-permute-done | bytes 5152 | tf_op jit(solution)/shard_map/ppermute | solution.py:18
  279.3 5.5 %collective-permute-done.3 = bf16[64,20,2]{2,0,1:T(8,128)(2,1)S(1)} collective-permute-done((bf16[64,20,2]{2,0,1:T(8,128)(2,1)S(1)}, bf16[64,20,2]{2,0,1:T(8,128)(2,1)S(1)}, u32[]{:S(2)}, u32[]{:S(2)}) %collective-permute-start.3) | collective-permute-done | bytes 5152 | tf_op jit(solution)/shard_map/ppermute | solution.py:20
  284.8 2.7 maximum_maximum_fusion
  287.5 18.1 %add_convert_fusion = bf16[64,16,1280]{2,0,1:T(8,128)(2,1)S(1)} fusion(bf16[64,16,1280]{2,0,1:T(8,128)(2,1)S(1)} %fusion.8, bf16[64,2,1280]{2,0,1:T(8,128)(2,1)S(1)} %collective-permute-done.1, bf16[64,20,1282]{2,0,1:T(8,128)(2,1)S(1)} %get-tuple-element.11, bf16[64,20,1282]{2,0,1:T(8,128)(2,1)S(1)} %get-tuple-element.10, ...), kind=kLoop, calls=%fused_computation.16 | loop fusion | flops 72089600 | bytes 38010880 | tf_op jit(solution)/shard_map/convert_element_type | solution.py:96
  305.6 2.9 copy.25
  (15 shorter events, 0.2 us)
Async XLA Ops:
  7.2 238.4 %all-gather.2.cloned.1.call-start = ((), (), s32[]{:S(2)}) async-start(), calls=%async_computation.2 | async-start | bytes 6553600 | tf_op jit(solution)/shard_map/all_gather | solution.py:76
  103.2 43.8 %copy-start.3 = (s32[1280]{0:T(1024)S(1)}, s32[1280]{0:T(1024)}, u32[]{:S(2)}) copy-start(s32[1280]{0:T(1024)} %param.8) | copy-start | bytes 15364
  255.5 15.6 %copy-start = (f32[2,16,1280]{2,1,0:T(8,128)S(1)}, f32[2,16,1280]{2,1,0:T(8,128)}, u32[]{:S(2)}) copy-start(f32[2,16,1280]{2,1,0:T(8,128)} %param.11) | copy-start | bytes 491524
  255.5 15.6 %copy-start.1 = (s32[16,1280]{1,0:T(8,128)S(1)}, s32[16,1280]{1,0:T(8,128)}, u32[]{:S(2)}) copy-start(s32[16,1280]{1,0:T(8,128)} %param.9) | copy-start | bytes 245764
  255.5 15.6 %copy-start.2 = (s32[16,1280]{1,0:T(8,128)S(1)}, s32[16,1280]{1,0:T(8,128)}, u32[]{:S(2)}) copy-start(s32[16,1280]{1,0:T(8,128)} %param.10) | copy-start | bytes 245764
  255.6 7.6 %collective-permute-start = (bf16[64,2,1280]{2,0,1:T(8,128)(2,1)S(1)}, bf16[64,2,1280]{2,0,1:T(8,128)(2,1)S(1)}, u32[]{:S(2)}, u32[]{:S(2)}) collective-permute-start(bf16[64,2,1280]{2,0,1:T(8,128)(2,1)S(1)} %get-tuple-element.14), channel_id=1, source_target_pairs={{0,4},{4,8},{8,12},{12,16},{16,20},{20,24},{24,28},{1,5},{5,9},{9,... | collective-permute-start | bytes 983048 | tf_op jit(solution)/shard_map/ppermute | solution.py:18
  259.2 8.4 %collective-permute-start.1 = (bf16[64,2,1280]{2,0,1:T(8,128)(2,1)S(1)}, bf16[64,2,1280]{2,0,1:T(8,128)(2,1)S(1)}, u32[]{:S(2)}, u32[]{:S(2)}) collective-permute-start(bf16[64,2,1280]{2,0,1:T(8,128)(2,1)S(1)} %get-tuple-element.15), channel_id=1, source_target_pairs={{4,0},{8,4},{12,8},{16,12},{20,16},{24,20},{28,24},{5,1},{9,5},{13... | collective-permute-start | bytes 983048 | tf_op jit(solution)/shard_map/ppermute | solution.py:20
  267.8 11.5 %collective-permute-start.2 = (bf16[64,20,2]{2,0,1:T(8,128)(2,1)S(1)}, bf16[64,20,2]{2,0,1:T(8,128)(2,1)S(1)}, u32[]{:S(2)}, u32[]{:S(2)}) collective-permute-start(bf16[64,20,2]{2,0,1:T(8,128)(2,1)S(1)} %get-tuple-element.12), channel_id=1, source_target_pairs={{0,1},{1,2},{2,3},{3,0},{4,5},{5,6},{6,7},{7,4},{8,9},{9,10},{10,1... | collective-permute-start | bytes 15368 | tf_op jit(solution)/shard_map/ppermute | solution.py:18
  267.8 16.9 %collective-permute-start.3 = (bf16[64,20,2]{2,0,1:T(8,128)(2,1)S(1)}, bf16[64,20,2]{2,0,1:T(8,128)(2,1)S(1)}, u32[]{:S(2)}, u32[]{:S(2)}) collective-permute-start(bf16[64,20,2]{2,0,1:T(8,128)(2,1)S(1)} %get-tuple-element.13), channel_id=1, source_target_pairs={{1,0},{2,1},{3,2},{0,3},{5,4},{6,5},{7,6},{4,7},{9,8},{10,9},{11,1... | collective-permute-start | bytes 15368 | tf_op jit(solution)/shard_map/ppermute | solution.py:20
Sparse Core Ops, SparseCore 0:
  147.2 98.3 all-gather.1
where the time goes:
time: 316 us; the launch traced here: 315 us
  waiting for transfers between devices  85.9 us (27%)
  blocking collectives  60.6 us (19%)
  local copies, waits for them, and re-layouts  58.5 us (19%)
  other arithmetic  57.8 us (18%)
  matrix products  29.6 us (9%)
  between operations  14.2 us (4%)
  starting transfers between devices  8.87 us (3%)
    all_gather x1, waiting for transfers between devices, per_device(): lax.all_gather(moved, 'lon', axis=3, tiled=True)  68.7 us
    all_to_all x1, blocking collectives, per_device(): lax.all_to_all(lax.all_to_all(fourier, 'lat', split_axis=1, concat_axis=0...  40.5 us
    another operation x1, other arithmetic  29.5 us
    unnamed x12, local copies, waits for them, and re-layouts  21.2 us
    all_to_all x1, blocking collectives, per_device(): lax.all_to_all(fourier, 'lat', split_axis=1, concat_axis=0, tiled=True)  20 us
    dot_general x1, matrix products, per_device(): jnp.einsum('mrbqn,mapn->mabprq', kept, matrices, preferred_element_type=j...  19.7 us
    convert_element_type x1, other arithmetic, per_device(): return (grid, total.astype(jnp.bfloat16))  18.1 us
    convert_element_type x1, local copies, waits for them, and re-layouts, per_device(): fourier = jnp.einsum('mrbqn,mapn->mabprq', kept, matrices, preferred_elem...  17.7 us
  transfers between devices with their start and end apart: 5, of which 5 were waited for; matrix products, arithmetic and copies ran while one was open for 10% of the time, Pallas kernels for 0%

commit v1 on v0

--- a/solution.py
+++ b/solution.py
@@ -1,3 +1,4 @@
+import functools
 import math
 import jax
 import jax.numpy as jnp
@@ -5,6 +6,18 @@
 from jax.sharding import PartitionSpec as P
 
 REACH = 1
+
+
+def run_inputs(field_in, axis_name):
+    return jnp.concatenate(
+        lax.all_to_all(
+            jnp.stack(jnp.split(field_in, lax.psum(1, axis_name), axis=1)), axis_name, 0, 0
+        ),
+        axis=0,
+    )
+
+
+_direct_waves = functools.partial(run_inputs, axis_name="lat")
 
 
 def padded_2(cells, sides, width, closed):
@@ -59,13 +72,7 @@
     fourier = jnp.einsum(
         "mrbqn,mapn->mabprq", kept, matrices, preferred_element_type=jnp.float32
     ).astype(jnp.bfloat16)
-    moved = lax.all_to_all(
-        lax.all_to_all(fourier, "lat", split_axis=1, concat_axis=0, tiled=True),
-        "lon",
-        split_axis=2,
-        concat_axis=0,
-        tiled=True,
-    )
+    moved = lax.all_to_all(_direct_waves(fourier), "lon", split_axis=2, concat_axis=0, tiled=True)
     wave_order = (
         wave_ids.reshape(lat_count, lon_parts, local_waves).transpose(1, 0, 2).reshape(all_waves)
     )

time: 316 us -> 336 us (1.063)
  local copies, waits for them, and re-layouts: 58.5 us -> 80.1 us
    another operation x0 -> x10, local copies, waits for them, and re-layouts: none -> 30.1 us  [run_inputs(): jnp.stack(jnp.split(field_in, lax.psum(1, axis_name), axis=1))]
    convert_element_type x1 -> x0, local copies, waits for them, and re-layouts: 17.7 us -> none  [per_device(): fourier = jnp.einsum('mrbqn,mapn->mabprq', kept, matrices, preferred_elem...]
    unnamed x12 -> x23, local copies, waits for them, and re-layouts: 21.2 us -> 31.2 us
    all_to_all x4 -> x2, local copies, waits for them, and re-layouts: 16.5 us -> 10.2 us  [the longest x1 9.03 us: run_inputs(): lax.all_to_all(jnp.stack(jnp.split(field_in, lax.psum(1, axis_name), axis...]
    reshape x0 -> x1, local copies, waits for them, and re-layouts: none -> 5.5 us  [run_inputs(): jnp.concatenate(lax.all_to_all(jnp.stack(jnp.split(field_in, lax.psum(1,...]
where the time goes in v1:
time: 336 us; the launch traced here: 335 us
  waiting for transfers between devices  85.6 us (25%)
  local copies, waits for them, and re-layouts  80.1 us (24%)
  blocking collectives  60.6 us (18%)
  other arithmetic  57.8 us (17%)
  matrix products  28.2 us (8%)
  between operations  14.3 us (4%)
  starting transfers between devices  8.87 us (3%)
    all_gather x1, waiting for transfers between devices, per_device(): lax.all_gather(moved, 'lon', axis=3, tiled=True)  68.7 us
    all_to_all x1, blocking collectives, per_device(): lax.all_to_all(_direct_waves(fourier), 'lon', split_axis=2, concat_axis=0...  40.5 us
    unnamed x23, local copies, waits for them, and re-layouts  31.2 us
    another operation x10, local copies, waits for them, and re-layouts, run_inputs(): jnp.stack(jnp.split(field_in, lax.psum(1, axis_name), axis=1))  30.1 us
    another operation x1, other arithmetic  29.6 us
    all_to_all x1, blocking collectives, run_inputs(): lax.all_to_all(jnp.stack(jnp.split(field_in, lax.psum(1, axis_name), axis...  20.1 us
    dot_general x1, matrix products, per_device(): jnp.einsum('mrbqn,mapn->mabprq', kept, matrices, preferred_element_type=j...  18.4 us
    convert_element_type x1, other arithmetic, per_device(): return (grid, total.astype(jnp.bfloat16))  18.1 us
  transfers between devices with their start and end apart: 5, of which 5 were waited for; matrix products, arithmetic and copies ran while one was open for 10% of the time, Pallas kernels for 0%

profile of v1, /device:TPU:5, one launch (start us, length us, event | category | flops | bytes accessed | tf_op | source)
XLA Modules:
  0.0 335.4 jit_solution(1477870000359007491)
XLA Ops:
  8.1 7.0 %broadcast_select_fusion = bf16[40,2,64,1280]{3,2,1,0:T(8,128)(2,1)S(1)} fusion(bf16[40,2,64,1280]{3,2,1,0:T(8,128)(2,1)} %param.6, pred[40,1280]{1,0:T(8,128)(4,1)S(1)} %iota_compare_fusion), kind=kLoop, calls=%fused_computation | loop fusion | flops 6553600 | bytes 26265600 | tf_op jit(solution)/shard_map/jit(_where)/select_n | solution.py:69
  15.1 18.4 %convert_bitcast_fusion = bf16[40,8,4,16,2,16]{3,5,1,2,4,0:T(8,128)(2,1)S(1)} fusion(bf16[40,2,4,16,1280,1]{4,3,5,2,1,0:T(8,128)(2,1)S(1)} %bitcast.104, bf16[40,8,16,1280,1,1]{3,2,1,5,4,0:T(8,128)(2,1)} %bitcast.109), kind=kOutput, calls=%fused_computation.1 | convolution fusion | flops 1678376960 | bytes 27525120 | tf_op jit(solution)/shard_map/mrbqn,mapn->mabprq/dot_general | solution.py:72
  33.5 4.3 %slice_bitcast_fusion = (bf16[1,40,1,4,16,2,16]{4,6,3,5,1,2,0:T(8,128)(2,1)S(1)}, bf16[1,40,1,4,16,2,16]{4,6,3,5,1,2,0:T(8,128)(2,1)}, bf16[1,40,1,4,16,2,16]{4,...) fusion(bf16[40,8,4,16,2,16]{3,5,1,2,4,0:T(8,128)(2,1)S(1)} %con, ...), kind=kLoop, calls=%fused_computation.25 | loop fusion | bytes 2621440 | tf_op jit(solution)/shard_map/stack | solution.py:14
  37.8 3.0 copy.52
  41.7 3.7 %copy.53 = bf16[1,40,1,4,16,2,16]{1,6,5,4,3,2,0:T(8,128)(2,1)} copy(bf16[1,40,1,4,16,2,16]{4,6,3,5,1,2,0:T(8,128)(2,1)} %get-tuple-element.18) | data formatting | bytes 327680 | tf_op jit(solution)/shard_map/stack | solution.py:14
  45.3 3.7 %copy.54 = bf16[1,40,1,4,16,2,16]{1,6,5,4,3,2,0:T(8,128)(2,1)} copy(bf16[1,40,1,4,16,2,16]{4,6,3,5,1,2,0:T(8,128)(2,1)} %get-tuple-element.17) | data formatting | bytes 327680 | tf_op jit(solution)/shard_map/stack | solution.py:14
  49.0 3.6 %copy.55 = bf16[1,40,1,4,16,2,16]{1,6,5,4,3,2,0:T(8,128)(2,1)} copy(bf16[1,40,1,4,16,2,16]{4,6,3,5,1,2,0:T(8,128)(2,1)} %get-tuple-element.16) | data formatting | bytes 327680 | tf_op jit(solution)/shard_map/stack | solution.py:14
  52.6 3.6 %copy.56 = bf16[1,40,1,4,16,2,16]{1,6,5,4,3,2,0:T(8,128)(2,1)} copy(bf16[1,40,1,4,16,2,16]{4,6,3,5,1,2,0:T(8,128)(2,1)} %get-tuple-element.15) | data formatting | bytes 327680 | tf_op jit(solution)/shard_map/stack | solution.py:14
  56.2 3.7 %copy.57 = bf16[1,40,1,4,16,2,16]{1,6,5,4,3,2,0:T(8,128)(2,1)} copy(bf16[1,40,1,4,16,2,16]{4,6,3,5,1,2,0:T(8,128)(2,1)} %get-tuple-element.14) | data formatting | bytes 327680 | tf_op jit(solution)/shard_map/stack | solution.py:14
  65.5 1.9 constant_dynamic-update-slice_fusion.5
  67.4 1.9 constant_dynamic-update-slice_fusion.4
  73.7 8.1 %reshape.249 = bf16[8,2,40960]{2,1,0:T(2,128)(2,1)S(1)} reshape(bf16[8,1,4,16,2,16,40]{6,5,4,3,2,1,0:T(8,128)(2,1)} %bitcast.107) | data formatting | bytes 2621440
  81.8 20.1 %all_to_all.20 = bf16[8,2,40960]{2,1,0:T(2,128)(2,1)S(1)} all-to-all(bf16[8,2,40960]{2,1,0:T(2,128)(2,1)S(1)} %reshape.249), channel_id=1, replica_groups=mesh['lat'=8,'lon'=4] {'lat'}, dimensions={0} | all-to-all | bytes 2621440 | tf_op jit(solution)/shard_map/all_to_all | solution.py:13
  101.9 7.2 %reshape.250 = bf16[8,1,4,16,2,16,40]{6,5,4,3,2,1,0:T(8,128)(2,1)} reshape(bf16[8,2,40960]{2,1,0:T(2,128)(2,1)S(1)} %all_to_all.20) | data formatting | bytes 2621440
  109.0 9.0 %copy.60 = bf16[8,40,1,4,16,2,16]{1,0,6,5,4,3,2:T(8,128)(2,1)} copy(bf16[8,40,1,4,16,2,16]{1,6,5,4,3,2,0:T(8,128)(2,1)} %bitcast.103) | data formatting | bytes 2621440 | tf_op jit(solution)/shard_map/all_to_all | solution.py:13
  118.1 5.5 %reshape.243 = bf16[320,1,4,16,2,16]{0,5,4,3,2,1:T(8,128)(2,1)S(1)} reshape(bf16[8,40,1,4,16,2,16]{1,0,6,5,4,3,2:T(8,128)(2,1)} %copy.60) | data formatting | bytes 2621440 | tf_op jit(solution)/shard_map/reshape | solution.py:12
  123.6 40.5 %all_to_all.21 = bf16[320,1,4,16,2,16]{0,5,4,3,1,2:T(8,128)(2,1)S(1)} all-to-all(bf16[320,1,4,16,2,16]{0,5,4,3,1,2:T(8,128)(2,1)S(1)} %bitcast.106), channel_id=1, replica_groups=mesh['lat'=8,'lon'=4] {'lon'}, dimensions={2} | all-to-all | bytes 2621440 | tf_op jit(solution)/shard_map/all_to_all | solution.py:75
  165.3 2.1 reshape.244
  167.6 29.6 %multiply_convert_fusion.1 = (bf16[1,1280,1280]{2,1,0:T(8,128)(2,1)S(1)}, bf16[1,1280,1280]{2,1,0:T(8,128)(2,1)}) fusion(s32[1280]{0:T(1024)S(1)} %iota_add_fusion, s32[1280]{0:T(1024)S(1)} %reshape.240, f32[1280]{0:T(1024)S(1)} %get-tuple-element.40, f32[1280]{0:T(1024)S(1)} %get-tuple-element.41), kind=kLoop, calls=%fused_computation.10 | loop fusion | flops 21299200 | bytes 6574080 | tf_op jit(solution)/shard_map/convert
  197.2 68.7 %all-gather.2.cloned.1.call-done = bf16[1280,16,2,64]{0,3,2,1:T(8,128)(2,1)} async-done(((bf16[1280,16,2,16]{0,3,2,1:T(8,128)(2,1)}), bf16[1280,16,2,64]{0,3,2,1:T(8,128)(2,1)}) %all-gather.2.cloned.1.call-update) | async-done | bytes 5242896 | tf_op jit(solution)/shard_map/all_gather | solution.py:83
  265.9 9.9 %fusion.8 = bf16[64,16,1280]{2,0,1:T(8,128)(2,1)S(1)} fusion(bf16[1280,16,2,64]{0,3,2,1:T(8,128)(2,1)} %all-gather.2.cloned.1.call-done, bf16[1,1280,1280]{2,1,0:T(8,128)(2,1)} %get-tuple-element.39, bf16[1,1280,1280]{2,1,0:T(8,128)(2,1)S(1)} %get-tuple-element.38), kind=kOutput, calls=%fused_computation.19 | convolution fusion | flops 6725304320 | bytes 14417920 | tf_op jit(solution)/shard_map/mprq,rmx->qpx/dot_general | solution.py:81
  275.9 3.6 %collective-permute-start = (bf16[64,2,1280]{2,0,1:T(8,128)(2,1)S(1)}, bf16[64,2,1280]{2,0,1:T(8,128)(2,1)S(1)}, u32[]{:S(2)}, u32[]{:S(2)}) collective-permute-start(bf16[64,2,1280]{2,0,1:T(8,128)(2,1)S(1)} %get-tuple-element.24), channel_id=1, source_target_pairs={{0,4},{4,8},{8,12},{12,16},{16,20},{20,24},{24,28},{1,5},{5,9},{9,... | collective-permute-start | bytes 983048 | tf_op jit(solution)/shard_map/ppermute | solution.py:31
  279.5 1.9 collective-permute-start.1
  281.4 2.1 collective-permute-done
  283.5 4.4 %collective-permute-done.1 = bf16[64,2,1280]{2,0,1:T(8,128)(2,1)S(1)} collective-permute-done((bf16[64,2,1280]{2,0,1:T(8,128)(2,1)S(1)}, bf16[64,2,1280]{2,0,1:T(8,128)(2,1)S(1)}, u32[]{:S(2)}, u32[]{:S(2)}) %collective-permute-start.1) | collective-permute-done | bytes 327712 | tf_op jit(solution)/shard_map/ppermute | solution.py:33
  288.2 3.3 collective-permute-start.3
  291.5 2.9 copy.63
  294.4 5.1 %collective-permute-done.2 = bf16[64,20,2]{2,0,1:T(8,128)(2,1)S(1)} collective-permute-done((bf16[64,20,2]{2,0,1:T(8,128)(2,1)S(1)}, bf16[64,20,2]{2,0,1:T(8,128)(2,1)S(1)}, u32[]{:S(2)}, u32[]{:S(2)}) %collective-permute-start.2) | collective-permute-done | bytes 5152 | tf_op jit(solution)/shard_map/ppermute | solution.py:31
  299.6 5.2 %collective-permute-done.3 = bf16[64,20,2]{2,0,1:T(8,128)(2,1)S(1)} collective-permute-done((bf16[64,20,2]{2,0,1:T(8,128)(2,1)S(1)}, bf16[64,20,2]{2,0,1:T(8,128)(2,1)S(1)}, u32[]{:S(2)}, u32[]{:S(2)}) %collective-permute-start.3) | collective-permute-done | bytes 5152 | tf_op jit(solution)/shard_map/ppermute | solution.py:33
  304.8 2.7 maximum_maximum_fusion
  307.5 18.1 %add_convert_fusion = bf16[64,16,1280]{2,0,1:T(8,128)(2,1)S(1)} fusion(bf16[64,16,1280]{2,0,1:T(8,128)(2,1)S(1)} %fusion.8, bf16[64,2,1280]{2,0,1:T(8,128)(2,1)S(1)} %collective-permute-done.1, bf16[64,20,1282]{2,0,1:T(8,128)(2,1)S(1)} %get-tuple-element.21, bf16[64,20,1282]{2,0,1:T(8,128)(2,1)S(1)} %get-tuple-element.20, ...), kind=kLoop, calls=%fused_computation.16 | loop fusion | flops 72089600 | bytes 38010880 | tf_op jit(solution)/shard_map/convert_element_type | solution.py:103
  325.7 2.9 copy.64
  (34 shorter events, 13.6 us)
Async XLA Ops:
  7.2 258.7 %all-gather.2.cloned.1.call-start = ((), (), s32[]{:S(2)}) async-start(), calls=%async_computation.2 | async-start | bytes 6553600 | tf_op jit(solution)/shard_map/all_gather | solution.py:83
  40.8 19.1 %copy-start = (bf16[1,40,1,4,16,2,16]{4,6,3,5,1,2,0:T(8,128)(2,1)S(1)}, bf16[1,40,1,4,16,2,16]{4,6,3,5,1,2,0:T(8,128)(2,1)}, u32[]{:S(2)}) copy-start(bf16[1,40,1,4,16,2,16]{4,6,3,5,1,2,0:T(8,128)(2,1)} %get-tuple-element.13) | copy-start | bytes 491524
  61.8 9.4 %copy-start.1 = (bf16[1,40,1,4,16,2,16]{1,6,5,4,3,2,0:T(8,128)(2,1)S(1)}, bf16[1,40,1,4,16,2,16]{1,6,5,4,3,2,0:T(8,128)(2,1)}, u32[]{:S(2)}) copy-start(bf16[1,40,1,4,16,2,16]{1,6,5,4,3,2,0:T(8,128)(2,1)} %copy.57) | copy-start | bytes 491524
  123.6 43.8 %copy-start.5 = (s32[1280]{0:T(1024)S(1)}, s32[1280]{0:T(1024)}, u32[]{:S(2)}) copy-start(s32[1280]{0:T(1024)} %param.8) | copy-start | bytes 15364
  275.8 15.6 %copy-start.2 = (f32[2,16,1280]{2,1,0:T(8,128)S(1)}, f32[2,16,1280]{2,1,0:T(8,128)}, u32[]{:S(2)}) copy-start(f32[2,16,1280]{2,1,0:T(8,128)} %param.11) | copy-start | bytes 491524
  275.8 15.6 %copy-start.3 = (s32[16,1280]{1,0:T(8,128)S(1)}, s32[16,1280]{1,0:T(8,128)}, u32[]{:S(2)}) copy-start(s32[16,1280]{1,0:T(8,128)} %param.9) | copy-start | bytes 245764
  275.8 15.6 %copy-start.4 = (s32[16,1280]{1,0:T(8,128)S(1)}, s32[16,1280]{1,0:T(8,128)}, u32[]{:S(2)}) copy-start(s32[16,1280]{1,0:T(8,128)} %param.10) | copy-start | bytes 245764
  275.9 7.6 %collective-permute-start = (bf16[64,2,1280]{2,0,1:T(8,128)(2,1)S(1)}, bf16[64,2,1280]{2,0,1:T(8,128)(2,1)S(1)}, u32[]{:S(2)}, u32[]{:S(2)}) collective-permute-start(bf16[64,2,1280]{2,0,1:T(8,128)(2,1)S(1)} %get-tuple-element.24), channel_id=1, source_target_pairs={{0,4},{4,8},{8,12},{12,16},{16,20},{20,24},{24,28},{1,5},{5,9},{9,... | collective-permute-start | bytes 983048 | tf_op jit(solution)/shard_map/ppermute | solution.py:31
  279.5 8.4 %collective-permute-start.1 = (bf16[64,2,1280]{2,0,1:T(8,128)(2,1)S(1)}, bf16[64,2,1280]{2,0,1:T(8,128)(2,1)S(1)}, u32[]{:S(2)}, u32[]{:S(2)}) collective-permute-start(bf16[64,2,1280]{2,0,1:T(8,128)(2,1)S(1)} %get-tuple-element.25), channel_id=1, source_target_pairs={{4,0},{8,4},{12,8},{16,12},{20,16},{24,20},{28,24},{5,1},{9,5},{13... | collective-permute-start | bytes 983048 | tf_op jit(solution)/shard_map/ppermute | solution.py:33
  288.1 11.5 %collective-permute-start.2 = (bf16[64,20,2]{2,0,1:T(8,128)(2,1)S(1)}, bf16[64,20,2]{2,0,1:T(8,128)(2,1)S(1)}, u32[]{:S(2)}, u32[]{:S(2)}) collective-permute-start(bf16[64,20,2]{2,0,1:T(8,128)(2,1)S(1)} %get-tuple-element.22), channel_id=1, source_target_pairs={{0,1},{1,2},{2,3},{3,0},{4,5},{5,6},{6,7},{7,4},{8,9},{9,10},{10,1... | collective-permute-start | bytes 15368 | tf_op jit(solution)/shard_map/ppermute | solution.py:31
  288.2 16.7 %collective-permute-start.3 = (bf16[64,20,2]{2,0,1:T(8,128)(2,1)S(1)}, bf16[64,20,2]{2,0,1:T(8,128)(2,1)S(1)}, u32[]{:S(2)}, u32[]{:S(2)}) collective-permute-start(bf16[64,20,2]{2,0,1:T(8,128)(2,1)S(1)} %get-tuple-element.23), channel_id=1, source_target_pairs={{1,0},{2,1},{3,2},{0,3},{5,4},{6,5},{7,6},{4,7},{9,8},{10,9},{11,1... | collective-permute-start | bytes 15368 | tf_op jit(solution)/shard_map/ppermute | solution.py:33
Sparse Core Ops, SparseCore 0:
  167.5 98.3 all-gather.1
